TPU v7x, 256 devices: a whole 4x4x8 slice. The times are simulated.
256 devices in a mesh: sec: 2 (over y_lo), dp: 8 (over x, y_hi), seq: 16 (over z, core).
Axes of the slice: x: 4, y: 4 (y_hi: 2, y_lo: 2; y = y_hi * 2 + y_lo), z: 8, core: 2. Of those that a mesh axis runs over, the one named last changes fastest.
Arguments:
- hidden: bfloat16 [256, 128, 2560], P(('sec', 'dp', 'seq')), may hold values from -24 to 24
- cond_shift: bfloat16 [256, 2560], P(('sec', 'dp', 'seq')), may hold values from -0.3125 to 0.3125
- cond_scale: bfloat16 [256, 2560], P(('sec', 'dp', 'seq')), may hold values from -1.75 to 1.75
- noisy: bfloat16 [256, 128, 256], P(('sec', 'dp', 'seq')), may hold values from -6 to 6
- noise_level: float32 [256], P(('sec', 'dp', 'seq')), may hold values from 0.2 to 1
- w_out: bfloat16 [2560, 256], replicated, may hold values from -0.125 to 0.125
- w_embed: bfloat16 [256, 2048], replicated, may hold values from -0.375 to 0.375
- w_root: bfloat16 [2, 2048], replicated, may hold values from -0.03125 to 0.03125
- w_qkv: bfloat16 [3, 2048, 2048], P(None, None, 'seq'), may hold values from -0.125 to 0.125
- w_proj: bfloat16 [2048, 512], P('seq'), may hold values from -0.125 to 0.125
- text_table: bfloat16 [49408, 512], P('seq'), may hold values from -6 to 6
- text_ids: int32 [32, 32], replicated, may hold values from 0 to 49407
- prompt_index: int32 [256], P(('sec', 'dp')), may hold values from 0 to 31
- reward_weight: float32 [256], P(('sec', 'dp')), may hold values from 1000 to 4000
Outputs:
- rewards: float32 [256], P(('sec', 'dp'))
- grad_w_out: float32 [2560, 256], P('seq')
- grad_hidden: bfloat16 [256, 128, 2560], P(('sec', 'dp', 'seq'))
All inputs are finite; a program needn't handle non-finite values.
Results may differ from a plain program's by a relative error of at most 0.017.
The roundings to bfloat16 on the way count: a program that leaves them out, or rounds other values in their place, can miss the bound.
Values may be sent and summed in bfloat16 or wider, within the bound.
No kernel may reach another device: no remote copies, remote signals or barrier semaphores. Data moves between devices by JAX's collectives and lax.ppermute only.
A program may use at most 128 MiB of HBM per device.

v0:
```python
import jax
import jax.numpy as jnp
from jax import lax
from jax.sharding import PartitionSpec as P

D_REW = 2048
HEADS = 16
PROMPTS = 32
normalizing_sharpness = 10.0
epsilon = 1e-06
highest = lax.Precision.HIGHEST


def rotate(angle, first, second):
    cosine = jnp.cos(angle)
    sine_term = jnp.sin(angle)
    return (cosine * first + sine_term * second, cosine * second - sine_term * first)


def suffix(values):
    return jnp.sum(values, axis=1, keepdims=True) - jnp.cumsum(values, axis=1)


def local_path(motion):
    spin = motion[..., 0]
    theta = jnp.cumsum(spin, axis=1) - spin
    step_east, step_north = rotate(theta, motion[..., 1], motion[..., 2])
    path_east = jnp.cumsum(step_east, axis=1) - step_east
    path_north = jnp.cumsum(step_north, axis=1) - step_north
    return (theta, path_east, path_north)


def embed(motion, root_east, root_north, w_embed, root_rows):
    emb = jnp.einsum(
        "cfe,ed->cfd", motion.astype(jnp.bfloat16), w_embed, preferred_element_type=jnp.float32
    )
    emb = emb + root_east[..., None] * root_rows[0] + root_north[..., None] * root_rows[1]
    scale_rms = jnp.sqrt(jnp.mean(emb * emb, axis=-1, keepdims=True) + epsilon)
    return (emb / scale_rms, scale_rms)


def unit_rows(vectors):
    length = jnp.sqrt(jnp.sum(vectors * vectors, axis=-1, keepdims=True) + epsilon)
    return (vectors / length, length)


def norm_grad(grad, normed, scale_rms):
    return (grad - normed * jnp.mean(grad * normed, axis=-1, keepdims=True)) / scale_rms


def motion_grad(d_emb, normed_e, scale_rms, motion, theta, embed_rows, root_rows):
    d_unemb = norm_grad(d_emb, normed_e, scale_rms)
    d_embedded = jnp.einsum("cfd,ed->cfe", d_unemb, embed_rows, precision=highest)
    grad_east = suffix(jnp.sum(d_unemb * root_rows[0], axis=-1))
    grad_north = suffix(jnp.sum(d_unemb * root_rows[1], axis=-1))
    vel_east = motion[..., 1]
    vel_north = motion[..., 2]
    d_east, d_north = rotate(-theta, grad_east, grad_north)
    cosine = jnp.cos(theta)
    sine_term = jnp.sin(theta)
    d_theta = grad_east * (cosine * vel_north - sine_term * vel_east) - grad_north * (
        cosine * vel_east + sine_term * vel_north
    )
    d_spin = suffix(d_theta)
    return d_embedded.at[..., 0].add(d_spin).at[..., 1].add(d_east).at[..., 2].add(d_north)


def local(
    hidden,
    cond_shift,
    cond_scale,
    noisy,
    noise_level,
    w_out,
    w_embed,
    w_root,
    w_qkv,
    w_proj,
    text_table,
    text_ids,
    prompt_index,
    reward_weight,
):
    clips_dev = hidden.shape[0]
    ways = lax.axis_size("seq")
    group = clips_dev * ways
    frames = hidden.shape[1]
    width_cols = w_qkv.shape[2]
    head_size = D_REW // HEADS
    heads_dev = width_cols // head_size
    root_rows = w_root.astype(jnp.float32)
    embed_rows = w_embed.astype(jnp.float32)
    vocab_rows = text_table.shape[0]
    local_ids = text_ids - lax.axis_index("seq") * vocab_rows
    inside = (local_ids >= 0) & (local_ids < vocab_rows)
    picked = jnp.take(text_table, jnp.clip(local_ids, 0, vocab_rows - 1), axis=0).astype(
        jnp.float32
    )
    text_part = jnp.sum(jnp.where(inside[..., None], picked, 0.0), axis=1)
    text_raw = lax.psum(text_part, "seq")
    text_unit, text_len = unit_rows(text_raw)
    hidden_f = hidden.astype(jnp.float32)
    centred = hidden_f - jnp.mean(hidden_f, axis=-1, keepdims=True)
    inv_std = lax.rsqrt(jnp.mean(centred * centred, axis=-1, keepdims=True) + epsilon)
    normed_h = centred * inv_std
    gain = 1.0 + cond_scale.astype(jnp.float32)[:, None, :]
    modulated = (normed_h * gain + cond_shift.astype(jnp.float32)[:, None, :]).astype(jnp.bfloat16)
    eps_pred = jnp.einsum("cfd,de->cfe", modulated, w_out, preferred_element_type=jnp.float32)
    level = noise_level[:, None, None]
    x_clean = noisy.astype(jnp.float32) - level * eps_pred
    theta, path_east, path_north = local_path(x_clean)
    normed_e, scale_rms = embed(x_clean, path_east, path_north, w_embed, root_rows)
    projected = jnp.einsum(
        "cfd,jdk->cfjk",
        lax.all_gather(normed_e.astype(jnp.bfloat16), "seq", axis=0, tiled=True),
        w_qkv,
        preferred_element_type=jnp.float32,
    )
    projected = projected.reshape(group, frames, 3, heads_dev, head_size)
    query_unit, query_len = unit_rows(projected[:, :, 0])
    key_unit, key_len = unit_rows(projected[:, :, 1])
    asking_vectors_group = query_unit.astype(jnp.bfloat16)
    lookup_vectors_group = key_unit.astype(jnp.bfloat16)
    value_b = projected[:, :, 2].astype(jnp.bfloat16)
    similarity_table = normalizing_sharpness * jnp.einsum(
        "cfhd,cghd->chfg",
        asking_vectors_group,
        lookup_vectors_group,
        preferred_element_type=jnp.float32,
    )
    expo = jnp.exp(similarity_table)
    focus_probabilities = expo / jnp.sum(expo, axis=-1, keepdims=True)
    attention_b = focus_probabilities.astype(jnp.bfloat16)
    column_mass = jnp.sum(attention_b, axis=2, dtype=jnp.float32)
    value_f = value_b.astype(jnp.float32)
    pooled = jnp.einsum("chg,cghd->chd", column_mass, value_f, precision=highest)
    pooled_b = pooled.astype(jnp.bfloat16).reshape(group, width_cols)
    motion_part = jnp.dot(pooled_b, w_proj, preferred_element_type=jnp.float32)
    motion_emb = lax.psum(motion_part, "seq")
    choose = (prompt_index[:, None] == jnp.arange(PROMPTS)[None, :]).astype(jnp.float32)
    target = jnp.dot(choose, text_unit, precision=highest)
    emb_len = jnp.sqrt(jnp.sum(motion_emb * motion_emb, axis=-1) + epsilon)
    rewards = jnp.sum(motion_emb * target, axis=-1) / emb_len
    d_memb = (
        (-reward_weight)[:, None]
        * (target - rewards[:, None] * motion_emb / emb_len[:, None])
        / emb_len[:, None]
    )
    d_pooled = jnp.dot(d_memb, w_proj.astype(jnp.float32).T, precision=highest).reshape(
        group, heads_dev, head_size
    )
    reduction_dimension = jnp.einsum("chd,cghd->chg", d_pooled, value_f, precision=highest)
    d_value = jnp.transpose(column_mass, (0, 2, 1))[..., None] * d_pooled[:, None]
    pairwise_dot_similarity = jnp.sum(
        focus_probabilities * reduction_dimension[:, :, None, :], axis=-1, keepdims=True
    )
    similarity_derivative = (
        normalizing_sharpness
        * focus_probabilities
        * (reduction_dimension[:, :, None, :] - pairwise_dot_similarity)
    ).astype(jnp.bfloat16)
    d_qu = jnp.einsum(
        "chfg,cghd->cfhd",
        similarity_derivative,
        lookup_vectors_group,
        preferred_element_type=jnp.float32,
    )
    d_ku = jnp.einsum(
        "chfg,cfhd->cghd",
        similarity_derivative,
        asking_vectors_group,
        preferred_element_type=jnp.float32,
    )
    d_query = (d_qu - query_unit * jnp.sum(query_unit * d_qu, axis=-1, keepdims=True)) / query_len
    d_key = (d_ku - key_unit * jnp.sum(key_unit * d_ku, axis=-1, keepdims=True)) / key_len
    d_proj = (
        jnp.stack([d_query, d_key, d_value], axis=2)
        .astype(jnp.bfloat16)
        .reshape(group, frames, 3, width_cols)
    )
    d_emb = lax.psum_scatter(
        jnp.einsum("cfjk,jdk->cfd", d_proj, w_qkv, preferred_element_type=jnp.float32),
        "seq",
        scatter_dimension=0,
        tiled=True,
    )
    d_motion = motion_grad(d_emb, normed_e, scale_rms, x_clean, theta, embed_rows, root_rows)
    d_eps_b = (-level * d_motion).astype(jnp.bfloat16)
    d_mod = jnp.einsum("cfe,de->cfd", d_eps_b, w_out, preferred_element_type=jnp.float32)
    d_norm = d_mod * gain
    grad_hidden = (
        inv_std
        * (
            d_norm
            - jnp.mean(d_norm, axis=-1, keepdims=True)
            - normed_h * jnp.mean(d_norm * normed_h, axis=-1, keepdims=True)
        )
    ).astype(jnp.bfloat16)
    rows_dev = w_out.shape[0] // ways
    grad_term = jnp.einsum("cfd,cfe->de", modulated, d_eps_b, preferred_element_type=jnp.float32)
    grad_total = lax.psum(grad_term, ("sec", "dp", "seq"))
    grad_w_out = lax.dynamic_slice_in_dim(grad_total, lax.axis_index("seq") * rows_dev, rows_dev, 0)
    return (rewards, grad_w_out, grad_hidden)


def solution(mesh):
    placed = (
        P(("sec", "dp", "seq"), None, None),
        P(("sec", "dp", "seq"), None),
        P(("sec", "dp", "seq"), None),
        P(("sec", "dp", "seq"), None, None),
        P(("sec", "dp", "seq")),
        P(),
        P(),
        P(),
        P(None, None, "seq"),
        P("seq", None),
        P("seq", None),
        P(),
        P(("sec", "dp")),
        P(("sec", "dp")),
    )
    return jax.shard_map(
        local,
        mesh=mesh,
        in_specs=placed,
        out_specs=(P(("sec", "dp")), P("seq", None), P(("sec", "dp", "seq"), None, None)),
        check_vma=False,
    )
```

profile of v0, /device:TPU:2, one launch (start us, length us, event | category | flops | bytes accessed | tf_op | source)
XLA Modules:
  0.0 640.3 jit_solution(5430359469314224564)
XLA Ops:
  7.2 0.9 compare_and_fusion
  8.2 0.9 copy-done
  9.1 5.1 gather_fusion
  14.2 2.3 select_reduce_fusion
  17.3 1.3 convert_reduce_fusion
  18.5 1.4 fusion.22
  20.0 0.6 fusion.77
  20.7 1.8 fusion.24
  22.5 0.8 slice_reduce_fusion.1
  23.8 0.5 copy-done.33
  25.1 0.6 subtract_reduce_fusion.1
  26.0 1.7 multiply_reduce_fusion.3
  27.8 0.9 copy-done.4
  28.7 0.9 fusion.74
  29.8 0.5 neg.19
  30.3 88.0 %all-reduce.3.cloned.1.call-done = f32[32,512]{1,0:T(8,128)} async-done(((f32[32,512]{1,0:T(8,128)}), f32[32,512]{1,0:T(8,128)}) %all-reduce.3.cloned.1.call-update) | async-done | bytes 65552 | tf_op jit(solution)/shard_map/psum | solution.py:100
  118.3 1.0 multiply_reduce_fusion.8
  119.3 0.5 add_sqrt_fusion.2
  119.8 55.7 %all-gather.3.cloned.1.call-done = bf16[2048,2048]{1,0:T(8,128)(2,1)} async-done(((bf16[128,2048]{1,0:T(8,128)(2,1)}), bf16[2048,2048]{1,0:T(8,128)(2,1)}) %all-gather.3.cloned.1.call-update) | async-done | bytes 8388624 | tf_op jit(solution)/shard_map/all_gather | solution.py:115
  175.5 6.4 convolution_bitcast_fusion.1
  182.1 1.6 fusion.32
  183.9 2.7 convert_reduce_fusion.1
  186.6 2.1 fusion.37
  188.8 47.4 %psum.21 = f32[16,512]{1,0:T(8,128)} all-reduce(f32[16,512]{1,0:T(8,128)S(1)} %fusion.59), channel_id=1, replica_groups=mesh['sec'=2,'dp'=8,'seq'=16] {'seq'}, use_global_device_ids=true, to_apply=%region_10.11 | all-reduce | flops 8192 | bytes 65536 | tf_op jit(solution)/shard_map/psum | solution.py:139
  236.2 1.2 multiply_reduce_fusion.9
  237.5 1.0 fusion.45
  238.4 0.4 multiply_convert_fusion
  238.8 1.7 fusion.35
  241.0 0.6 convolution_bitcast_fusion.2
  241.5 1.0 copy-done.2
  242.7 0.8 multiply_reduce_fusion.1
  243.4 0.6 divide_convert_fusion.1
  244.0 0.8 copy-done.9
  244.8 8.1 %convolution_bitcast_fusion = f32[16,128,2048]{2,1,0:T(8,128)} fusion(bf16[16,128,1,128]{1,3,0,2:T(8,128)(2,1)S(1)} %multiply_convert_fusion, bf16[16,128,1,128]{1,3,0,2:T(8,128)(2,1)S(1)} %get-tuple-element.60, bf16[16,128,1,128]{1,3,0,2:T(8,128)(2,1)S(1)} %get-tuple-element.59, bf16[3,2048,128]{2,1,0:T(8,128)(2,1)S(1)} %copy-done.9), kind=kOutput, calls=%fused_computation.2 | convolution fusion | flops 3222798336 | bytes 19922944 | tf_op jit(solution)/shard_map/cfjk,jdk->cfd/dot_general | solution.py:182
  253.2 100.2 %reduce-scatter.2.cloned.1.call-done = f32[1,128,2048]{2,1,0:T(8,128)} async-done(((f32[16,128,2048]{2,1,0:T(8,128)}), f32[1,128,2048]{2,1,0:T(8,128)}) %reduce-scatter.2.cloned.1.call-update) | async-done | bytes 1048592 | tf_op jit(solution)/shard_map/reduce_scatter | solution.py:181
  353.5 1.9 fusion.30
  355.7 2.1 multiply_reduce_fusion.7
  358.4 2.0 fusion.66
  360.8 2.7 fusion.27
  363.6 1.3 fusion.40
  364.9 1.0 scatter-add.10
  367.2 3.3 fusion.53
  370.5 0.7 copy-done.15
  371.2 3.2 fusion.18
  374.3 1.5 reduce_sum.224
  375.8 2.8 fusion.21
  378.7 253.5 %all-reduce.5.cloned.1.call-done = f32[2560,256]{1,0:T(8,128)} async-done(((f32[2560,256]{1,0:T(8,128)}), f32[2560,256]{1,0:T(8,128)}) %all-reduce.5.cloned.1.call-update) | async-done | bytes 2621456 | tf_op jit(solution)/shard_map/psum | solution.py:201
  632.2 1.6 constant_dynamic-slice_fusion
  (110 shorter events, 5.8 us)
Async XLA Ops:
  7.2 1.9 copy-start
  7.2 111.1 %all-reduce.3.cloned.1.call-start = ((), (), s32[]{:S(2)}) async-start(), calls=%async_computation.1 | async-start | bytes 131072 | tf_op jit(solution)/shard_map/psum | solution.py:100
  14.1 5.8 copy-start.20
  14.1 6.4 %copy-start.21 = (bf16[1,2560]{1,0:T(2,128)(2,1)S(1)}, bf16[1,2560]{1,0:T(2,128)(2,1)}, u32[]{:S(2)}) copy-start(bf16[1,2560]{1,0:T(2,128)(2,1)} %param.21) | copy-start | bytes 15364
  14.1 6.4 %copy-start.22 = (bf16[1,2560]{1,0:T(2,128)(2,1)S(1)}, bf16[1,2560]{1,0:T(2,128)(2,1)}, u32[]{:S(2)}) copy-start(bf16[1,2560]{1,0:T(2,128)(2,1)} %param.22) | copy-start | bytes 15364
  14.2 6.5 %copy-start.36 = (bf16[1,128,256]{2,1,0:T(8,128)(2,1)S(1)}, bf16[1,128,256]{2,1,0:T(8,128)(2,1)}, u32[]{:S(2)}) copy-start(bf16[1,128,256]{2,1,0:T(8,128)(2,1)} %param.23) | copy-start | bytes 196612
  16.5 159.0 %all-gather.3.cloned.1.call-start = ((), (), s32[]{:S(2)}) async-start(), calls=%async_computation.4 | async-start | bytes 8912896 | tf_op jit(solution)/shard_map/all_gather | solution.py:115
  16.5 4.1 copy-start.3
  18.5 3.9 copy-start.23
  20.0 2.5 copy-start.27
  20.7 1.8 copy-start.14
  20.7 1.8 copy-start.17
  23.3 0.6 copy-start.31
  23.8 0.5 copy-start.33
  24.9 2.8 copy-start.10
  27.7 1.0 copy-start.4
  27.8 2.0 copy-start.37
  27.8 1.0 copy-start.25
  29.7 323.8 %reduce-scatter.2.cloned.1.call-start = ((), (), s32[]{:S(2)}) async-start(), calls=%async_computation.2 | async-start | bytes 17825792 | tf_op jit(solution)/shard_map/reduce_scatter | solution.py:181
  181.9 2.0 copy-start.1
  183.9 4.8 copy-start.13
  183.9 52.3 %copy-start.16 = (f32[32,512]{1,0:T(8,128)S(1)}, f32[32,512]{1,0:T(8,128)}, u32[]{:S(2)}) copy-start(f32[32,512]{1,0:T(8,128)} %all-reduce.3.cloned.1.call-done) | copy-start | bytes 196612
  236.2 4.4 copy-start.6
  237.4 3.5 copy-start.35
  238.4 2.5 copy-start.8
  240.6 1.9 copy-start.2
  241.0 1.7 copy-start.12
  243.4 1.4 copy-start.9
  253.0 100.5 %copy-start.26 = (f32[128]{0:T(128)S(1)}, f32[128]{0:T(128)}, u32[]{:S(2)}) copy-start(f32[128]{0:T(128)} %copy-done.25) | copy-start | bytes 1540
  253.0 102.5 %copy-start.19 = (f32[1,2048]{1,0:T(1,128)S(1)}, f32[1,2048]{1,0:T(1,128)}, u32[]{:S(2)}) copy-start(f32[1,2048]{1,0:T(1,128)} %get-tuple-element.67) | copy-start | bytes 24580
  253.0 102.5 %copy-start.18 = (f32[1,2048]{1,0:T(1,128)S(1)}, f32[1,2048]{1,0:T(1,128)}, u32[]{:S(2)}) copy-start(f32[1,2048]{1,0:T(1,128)} %get-tuple-element.66) | copy-start | bytes 24580
  253.0 379.2 %all-reduce.5.cloned.1.call-start = ((), (), s32[]{:S(2)}) async-start(), calls=%async_computation.3 | async-start | bytes 5242880 | tf_op jit(solution)/shard_map/psum | solution.py:201
  353.5 2.0 copy-start.5
  353.5 2.2 copy-start.7
  355.6 2.7 copy-start.29
  355.6 2.7 copy-start.30
  355.6 2.7 copy-start.32
  355.6 2.7 copy-start.34
  355.6 5.0 copy-start.11
  370.5 0.7 copy-start.15
  370.5 0.7 copy-start.24
  370.5 0.7 copy-start.28
Sparse Core Ops, SparseCore 0:
  16.6 101.6 all-reduce.2
  120.9 54.6 all-gather.2
  253.1 100.3 reduce-scatter.1
  370.6 261.4 all-reduce.4
where the time goes:
time: 641 us; the launch traced here: 640 us
  waiting for transfers between devices  498 us (78%)
  blocking collectives  47.4 us (7%)
  matrix products  37.3 us (6%)
  other arithmetic  26.9 us (4%)
  local copies, waits for them, and re-layouts  15.9 us (2%)
  between operations  14.9 us (2%)
    psum x1, waiting for transfers between devices, local(): grad_total = lax.psum(grad_term, ('sec', 'dp', 'seq'))  253 us
    reduce_scatter x1, waiting for transfers between devices, local(): lax.psum_scatter(jnp.einsum('cfjk,jdk->cfd', d_proj, w_qkv, preferred_ele...  100 us
    psum x1, waiting for transfers between devices, local(): text_raw = lax.psum(text_part, 'seq')  88 us
    all_gather x1, waiting for transfers between devices, local(): lax.all_gather(normed_e.astype(jnp.bfloat16), 'seq', axis=0, tiled=True)  55.7 us
    psum x1, blocking collectives, local(): motion_emb = lax.psum(motion_part, 'seq')  47.4 us
  transfers between devices with their start and end apart: 4, of which 4 were waited for; matrix products, arithmetic and copies ran while one was open for 3% of the time, Pallas kernels for 0%

commit v1 on v0

--- a/solution.py
+++ b/solution.py
@@ -112,7 +112,12 @@
     normed_e, scale_rms = embed(x_clean, path_east, path_north, w_embed, root_rows)
     projected = jnp.einsum(
         "cfd,jdk->cfjk",
-        lax.all_gather(normed_e.astype(jnp.bfloat16), "seq", axis=0, tiled=True),
+        jnp.concatenate(
+            lax.all_to_all(
+                jnp.stack([normed_e.astype(jnp.bfloat16)] * lax.axis_size("seq")), "seq", 0, 0
+            ),
+            axis=0,
+        ),
         w_qkv,
         preferred_element_type=jnp.float32,
     )

time: 641 us -> 695 us (1.084)
  waiting for transfers between devices: 498 us -> 542 us
  starting transfers between devices: 0.34 us -> 8.88 us
    psum x1, waiting for transfers between devices: 88 us -> 187 us  [local(): text_raw = lax.psum(text_part, 'seq')]
    all_gather x1 -> x0, waiting for transfers between devices: 55.7 us -> none  [local(): lax.all_gather(normed_e.astype(jnp.bfloat16), 'seq', axis=0, tiled=True)]
    all_to_all x0 -> x1, starting transfers between devices: none -> 8.75 us  [local(): lax.all_to_all(jnp.stack([normed_e.astype(jnp.bfloat16)] * lax.axis_size(...]
  transfers between devices with their start and end apart: 4 -> 4, of which waited for: 4 -> 3; matrix products, arithmetic and copies ran while one was open for 3% -> 2% of each run, Pallas kernels for 0% -> 0%
where the time goes in v1:
time: 695 us; the launch traced here: 694 us
  waiting for transfers between devices  542 us (78%)
  blocking collectives  46.5 us (7%)
  matrix products  37.3 us (5%)
  other arithmetic  25.3 us (4%)
  local copies, waits for them, and re-layouts  19.3 us (3%)
  between operations  15.1 us (2%)
  starting transfers between devices  8.88 us (1%)
    psum x1, waiting for transfers between devices, local(): grad_total = lax.psum(grad_term, ('sec', 'dp', 'seq'))  253 us
    psum x1, waiting for transfers between devices, local(): text_raw = lax.psum(text_part, 'seq')  187 us
    reduce_scatter x1, waiting for transfers between devices, local(): lax.psum_scatter(jnp.einsum('cfjk,jdk->cfd', d_proj, w_qkv, preferred_ele...  101 us
    psum x1, blocking collectives, local(): motion_emb = lax.psum(motion_part, 'seq')  46.5 us
  transfers between devices with their start and end apart: 4, of which 3 were waited for; matrix products, arithmetic and copies ran while one was open for 2% of the time, Pallas kernels for 0%

profile of v1, /device:TPU:2, one launch (start us, length us, event | category | flops | bytes accessed | tf_op | source)
XLA Modules:
  0.0 694.0 jit_solution(10752710417186494003)
XLA Ops:
  8.0 1.4 convert_reduce_fusion
  9.4 1.4 fusion.27
  10.8 0.6 fusion.82
  11.6 1.8 fusion.29
  13.4 0.8 slice_reduce_fusion.1
  14.7 0.5 copy-done.34
  16.0 0.6 subtract_reduce_fusion.1
  16.9 1.7 multiply_reduce_fusion.3
  18.6 1.0 copy-done.4
  19.8 4.3 stack.4
  24.0 8.8 %all-to-all-start = ((bf16[16,1,128,2048]{3,2,1,0:T(8,128)(2,1)}), bf16[16,1,128,2048]{3,2,1,0:T(8,128)(2,1)}, u32[]{:S(2)}, u32[]{:S(2)}) async-start(bf16[16,1,128,2048]{3,2,1,0:T(8,128)(2,1)} %stack.4), calls=%async_computation | async-start | bytes 16777216 | tf_op jit(solution)/shard_map/all_to_all | solution.py:116
  33.0 5.1 gather_fusion
  38.0 2.2 select_reduce_fusion
  40.4 0.5 neg.19
  40.9 186.8 %all-reduce.3.cloned.1.call-done = f32[32,512]{1,0:T(8,128)} async-done(((f32[32,512]{1,0:T(8,128)}), f32[32,512]{1,0:T(8,128)}) %all-reduce.3.cloned.1.call-update) | async-done | bytes 65552 | tf_op jit(solution)/shard_map/psum | solution.py:100
  227.7 1.0 multiply_reduce_fusion.8
  228.7 0.5 add_sqrt_fusion.2
  229.2 6.4 fusion.4
  235.8 1.6 fusion.37
  237.6 2.7 convert_reduce_fusion.1
  240.3 2.1 fusion.42
  242.5 46.5 %psum.21 = f32[16,512]{1,0:T(8,128)} all-reduce(f32[16,512]{1,0:T(8,128)S(1)} %fusion.64), channel_id=1, replica_groups=mesh['sec'=2,'dp'=8,'seq'=16] {'seq'}, use_global_device_ids=true, to_apply=%region_10.11 | all-reduce | flops 8192 | bytes 65536 | tf_op jit(solution)/shard_map/psum | solution.py:144
  289.0 1.2 multiply_reduce_fusion.9
  290.3 1.0 fusion.50
  291.2 0.4 multiply_convert_fusion
  291.6 1.7 fusion.40
  293.8 0.6 convolution_bitcast_fusion.1
  294.3 1.0 copy-done.2
  295.5 0.8 multiply_reduce_fusion.1
  296.2 0.6 divide_convert_fusion.1
  296.8 0.8 copy-done.9
  297.6 8.1 %convolution_bitcast_fusion = f32[16,128,2048]{2,1,0:T(8,128)} fusion(bf16[16,128,1,128]{1,3,0,2:T(8,128)(2,1)S(1)} %multiply_convert_fusion, bf16[16,128,1,128]{1,3,0,2:T(8,128)(2,1)S(1)} %get-tuple-element.60, bf16[16,128,1,128]{1,3,0,2:T(8,128)(2,1)S(1)} %get-tuple-element.59, bf16[3,2048,128]{2,1,0:T(8,128)(2,1)S(1)} %copy-done.9), kind=kOutput, calls=%fused_computation.4 | convolution fusion | flops 3222798336 | bytes 19922944 | tf_op jit(solution)/shard_map/cfjk,jdk->cfd/dot_general | solution.py:187
  305.8 101.4 %reduce-scatter.2.cloned.1.call-done = f32[1,128,2048]{2,1,0:T(8,128)} async-done(((f32[16,128,2048]{2,1,0:T(8,128)}), f32[1,128,2048]{2,1,0:T(8,128)}) %reduce-scatter.2.cloned.1.call-update) | async-done | bytes 1048592 | tf_op jit(solution)/shard_map/reduce_scatter | solution.py:186
  407.3 1.9 fusion.35
  409.4 2.1 multiply_reduce_fusion.7
  412.2 2.0 fusion.71
  414.6 2.7 fusion.32
  417.4 1.3 fusion.45
  418.7 1.0 scatter-add.10
  420.0 0.4 scatter-add.11
  420.6 0.4 scatter-add.14
  421.0 3.3 fusion.58
  424.3 0.7 copy-done.15
  425.0 3.2 fusion.23
  428.1 1.5 reduce_sum.224
  429.6 2.8 fusion.26
  432.4 253.4 %all-reduce.5.cloned.1.call-done = f32[2560,256]{1,0:T(8,128)} async-done(((f32[2560,256]{1,0:T(8,128)}), f32[2560,256]{1,0:T(8,128)}) %all-reduce.5.cloned.1.call-update) | async-done | bytes 2621456 | tf_op jit(solution)/shard_map/psum | solution.py:206
  685.9 1.6 constant_dynamic-slice_fusion
  (112 shorter events, 5.0 us)
Async XLA Ops:
  7.2 25.8 %copy-start = (bf16[3088,512]{1,0:T(8,128)(2,1)S(1)}, bf16[3088,512]{1,0:T(8,128)(2,1)}, u32[]{:S(2)}) copy-start(bf16[3088,512]{1,0:T(8,128)(2,1)} %param.30) | copy-start | bytes 9486340
  7.2 4.4 copy-start.3
  7.2 3.6 copy-start.20
  7.2 4.2 copy-start.23
  7.2 4.2 copy-start.22
  7.2 4.3 copy-start.37
  9.4 3.9 copy-start.24
  10.8 2.5 copy-start.28
  11.5 1.8 copy-start.14
  11.5 1.8 copy-start.17
  14.1 0.6 copy-start.32
  14.7 0.5 copy-start.34
  15.8 2.8 copy-start.10
  18.6 1.0 copy-start.4
  18.6 1.1 copy-start.26
  24.0 8.8 %copy-start.21 = (s32[32,32]{1,0:T(8,128)S(1)}, s32[32,32]{1,0:T(8,128)}, u32[]{:S(2)}) copy-start(s32[32,32]{1,0:T(8,128)} %param.31) | copy-start | bytes 12292
  24.0 205.2 %all-to-all-start = ((bf16[16,1,128,2048]{3,2,1,0:T(8,128)(2,1)}), bf16[16,1,128,2048]{3,2,1,0:T(8,128)(2,1)}, u32[]{:S(2)}, u32[]{:S(2)}) async-start(bf16[16,1,128,2048]{3,2,1,0:T(8,128)(2,1)} %stack.4), calls=%async_computation | async-start | bytes 16777216 | tf_op jit(solution)/shard_map/all_to_all | solution.py:116
  32.8 194.9 %all-reduce.3.cloned.1.call-start = ((), (), s32[]{:S(2)}) async-start(), calls=%async_computation.2 | async-start | bytes 131072 | tf_op jit(solution)/shard_map/psum | solution.py:100
  33.0 7.4 %copy-start.38 = (f32[16]{0:T(128)S(1)}, f32[16]{0:T(128)}, u32[]{:S(2)}) copy-start(f32[16]{0:T(128)} %param.33) | copy-start | bytes 196
  40.3 366.9 %reduce-scatter.2.cloned.1.call-start = ((), (), s32[]{:S(2)}) async-start(), calls=%async_computation.3 | async-start | bytes 17825792 | tf_op jit(solution)/shard_map/reduce_scatter | solution.py:186
  235.6 2.0 copy-start.1
  237.6 4.8 copy-start.13
  237.6 51.4 %copy-start.16 = (f32[32,512]{1,0:T(8,128)S(1)}, f32[32,512]{1,0:T(8,128)}, u32[]{:S(2)}) copy-start(f32[32,512]{1,0:T(8,128)} %all-reduce.3.cloned.1.call-done) | copy-start | bytes 196612
  289.0 4.4 copy-start.6
  290.2 3.5 copy-start.36
  291.2 2.5 copy-start.8
  293.4 1.9 copy-start.2
  293.8 1.7 copy-start.12
  296.2 1.4 copy-start.9
  305.8 101.5 %copy-start.27 = (f32[128]{0:T(128)S(1)}, f32[128]{0:T(128)}, u32[]{:S(2)}) copy-start(f32[128]{0:T(128)} %copy-done.26) | copy-start | bytes 1540
  305.8 103.5 %copy-start.19 = (f32[1,2048]{1,0:T(1,128)S(1)}, f32[1,2048]{1,0:T(1,128)}, u32[]{:S(2)}) copy-start(f32[1,2048]{1,0:T(1,128)} %get-tuple-element.67) | copy-start | bytes 24580
  305.8 103.4 %copy-start.18 = (f32[1,2048]{1,0:T(1,128)S(1)}, f32[1,2048]{1,0:T(1,128)}, u32[]{:S(2)}) copy-start(f32[1,2048]{1,0:T(1,128)} %get-tuple-element.66) | copy-start | bytes 24580
  305.8 380.1 %all-reduce.5.cloned.1.call-start = ((), (), s32[]{:S(2)}) async-start(), calls=%async_computation.4 | async-start | bytes 5242880 | tf_op jit(solution)/shard_map/psum | solution.py:206
  407.3 2.0 copy-start.5
  407.3 2.2 copy-start.7
  409.4 2.7 copy-start.30
  409.4 2.7 copy-start.31
  409.4 2.7 copy-start.33
  409.4 2.7 copy-start.35
  409.4 5.0 copy-start.11
  424.3 0.7 copy-start.15
  424.3 0.7 copy-start.25
  424.3 0.7 copy-start.29
Sparse Core Ops, SparseCore 0:
  40.4 187.2 all-reduce.2
  305.9 101.2 reduce-scatter.1
  424.4 261.4 all-reduce.4
